TPU v7x, 32 devices: a whole 2x2x4 slice. The times are simulated.
32 devices in a mesh: dp: 2 (over x), expert: 4 (over y, core), tensor: 4 (over z).
Axes of the slice: x: 2, y: 2, z: 4, core: 2. Of those that a mesh axis runs over, the one named last changes fastest.
Arguments:
- output_grad: bfloat16 [2048, 4096], P(('dp', 'expert'), 'tensor'), may hold values from -6 to 6
- expert_ids: int32 [2048, 2], P(('dp', 'expert')), may hold values from 0 to 3, all different within a row; in each aligned block of 256 rows (0 to 255, 256 to 511, ...) at most 192 rows name the same one
- router_weights: bfloat16 [2048, 2], P(('dp', 'expert')), may hold values from 0.099609375 to 0.8984375
- gate_preact: bfloat16 [4, 1536, 14336], P('expert', 'dp', 'tensor'), may hold values from -6 to 6
- up_preact: bfloat16 [4, 1536, 14336], P('expert', 'dp', 'tensor'), may hold values from -6 to 6
- down_weight: bfloat16 [4, 14336, 4096], P('expert', 'tensor', 'dp'), may hold values from -0.046875 to 0.046875
Outputs:
- gate_preact_grad: bfloat16 [4, 1536, 14336], P('expert', 'dp', 'tensor')
- up_preact_grad: bfloat16 [4, 1536, 14336], P('expert', 'dp', 'tensor')
- down_grad: bfloat16 [4, 14336, 4096], P('expert', 'tensor', 'dp')
- router_grad: float32 [2048, 2], P(('dp', 'expert'))
Inputs may be any that keep to these rules, and one draw needn't show every extreme that they name: `expert_ids`: the ids of one token differ. Among the 256 rows of one device no expert is named by more than 192 rows, and in every draw some expert is named by exactly 192 rows of some device.
All inputs are finite; a program needn't handle non-finite values.
Results may differ from a plain program's by a relative error of at most 0.007.
Values may be sent and summed in bfloat16 or wider, within the bound.
No kernel may reach another device: no remote copies, remote signals or barrier semaphores. Data moves between devices by JAX's collectives and lax.ppermute only.
A program may use at most 192 MiB of HBM per device.

v0:
```python
import jax
import jax.numpy as jnp
from jax import lax
from jax.sharding import PartitionSpec as P

PARTIAL_DTYPE = jnp.float32


def silu_parts(values):
    sigma = jax.nn.sigmoid(values)
    return (values * sigma, sigma * (1.0 + values * (1.0 - sigma)))


def swap_dp(value):
    return lax.ppermute(value, "dp", perm=[(0, 1), (1, 0)])


def local(output_grad, expert_ids, router_weights, gate_preact, up_preact, down_weight):
    expert_count = lax.axis_size("expert")
    tensor_count = lax.axis_size("tensor")
    replica = lax.axis_index("dp")
    part = lax.axis_index("tensor")
    tokens_here = expert_ids.shape[0]
    choices_each = expert_ids.shape[1]
    capacity = gate_preact.shape[1] // expert_count
    flat_ids = expert_ids.reshape(-1)
    one_hot = (flat_ids[:, None] == jnp.arange(expert_count, dtype=jnp.int32)).astype(jnp.int32)
    earlier = jnp.cumsum(one_hot, axis=0) - one_hot
    slot_index = jnp.sum(earlier * one_hot, axis=1)
    target = (flat_ids * capacity + slot_index).reshape(tokens_here, choices_each)
    columns = jnp.arange(expert_count * capacity, dtype=jnp.int32)
    matches = [target[:, which][:, None] == columns[None, :] for which in range(choices_each)]
    selector = jnp.zeros((tokens_here, expert_count * capacity), jnp.bfloat16)
    gate_table = jnp.zeros((tokens_here, expert_count * capacity), jnp.float32)
    for which in range(choices_each):
        selector = jnp.where(matches[which], jnp.bfloat16(1.0), selector)
        gate_table = jnp.where(
            matches[which], router_weights[:, which : which + 1].astype(jnp.float32), gate_table
        )
    gate_send = jnp.sum(gate_table, axis=0).astype(jnp.bfloat16).reshape(expert_count, capacity)
    gate_float = gate_preact[0].astype(jnp.float32)
    up_float = up_preact[0].astype(jnp.float32)
    active, slope = silu_parts(gate_float)
    hidden = (active * up_float).astype(jnp.bfloat16)
    contract_rows = (((0,), (0,)), ((), ()))
    contract_cols = (((1,), (1,)), ((), ()))
    outgoing = lax.dot_general(
        selector, output_grad, contract_rows, preferred_element_type=jnp.float32
    )
    outgoing = outgoing.astype(jnp.bfloat16).reshape(expert_count, capacity, -1)
    hidden, outgoing = lax.optimization_barrier((hidden, outgoing))
    hidden_other = swap_dp(hidden)
    received = lax.all_to_all(outgoing, "expert", split_axis=0, concat_axis=0, tiled=True)
    gate_slots = lax.all_to_all(gate_send, "expert", split_axis=0, concat_axis=0, tiled=True)
    slots = expert_count * capacity
    narrow_rows = received.reshape(slots, -1)
    gate_bf16 = gate_slots.reshape(-1)
    gate_column = gate_bf16.astype(jnp.float32)[:, None]
    fragment = lax.all_gather(narrow_rows, "tensor", axis=1, tiled=True)
    width = fragment.shape[1]
    half = width // 2
    piece = half // tensor_count
    own_rows = lax.dynamic_slice_in_dim(fragment, replica * half, half, axis=1)
    send_rows = lax.dynamic_slice_in_dim(
        fragment, (1 - replica) * half + part * piece, piece, axis=1
    )
    other_piece = swap_dp(send_rows)
    other_rows = lax.all_gather(other_piece, "tensor", axis=1, tiled=True)
    hidden_other, other_rows = lax.optimization_barrier((hidden_other, other_rows))
    other_gates = swap_dp(gate_bf16).astype(jnp.float32)[:, None]
    local_weight = down_weight[0]
    partial_other = lax.dot_general(
        other_rows, local_weight, contract_cols, preferred_element_type=jnp.float32
    )
    partial_back = swap_dp(partial_other.astype(PARTIAL_DTYPE)).astype(jnp.float32)
    partial_own = lax.dot_general(
        own_rows, local_weight, contract_cols, preferred_element_type=jnp.float32
    )
    scaled_own = (gate_column * own_rows.astype(jnp.float32)).astype(jnp.bfloat16)
    scaled_other = (other_gates * other_rows.astype(jnp.float32)).astype(jnp.bfloat16)
    grad_own = lax.dot_general(
        hidden, scaled_own, contract_rows, preferred_element_type=jnp.float32
    )
    grad_other = lax.dot_general(
        hidden_other, scaled_other, contract_rows, preferred_element_type=jnp.float32
    )
    rounded_own = lax.optimization_barrier(grad_own.astype(jnp.bfloat16))
    rounded_other = lax.optimization_barrier(grad_other.astype(jnp.bfloat16))
    partial_back, rounded_own, rounded_other = lax.optimization_barrier(
        (partial_back, rounded_own, rounded_other)
    )
    upstream = partial_own + partial_back
    down_grad = (rounded_own.astype(jnp.float32) + rounded_other.astype(jnp.float32)).astype(
        jnp.bfloat16
    )
    score = jnp.sum(hidden.astype(jnp.float32) * upstream, axis=1)
    hidden_grad = gate_column * upstream
    gate_grad = (hidden_grad * up_float * slope).astype(jnp.bfloat16)
    up_grad = (hidden_grad * active).astype(jnp.bfloat16)
    summed_scores = lax.psum(score, "tensor")
    returned = lax.all_to_all(
        summed_scores.reshape(expert_count, capacity),
        "expert",
        split_axis=0,
        concat_axis=0,
        tiled=True,
    )
    flat_scores = returned.reshape(-1)
    router_grad = jnp.stack(
        [
            jnp.sum(jnp.where(matches[which], flat_scores[None, :], 0.0), axis=1)
            for which in range(choices_each)
        ],
        axis=1,
    )
    return (gate_grad[None], up_grad[None], down_grad[None], router_grad)


def solution(mesh):
    placed = (
        P(("dp", "expert"), "tensor"),
        P(("dp", "expert"), None),
        P(("dp", "expert"), None),
        P("expert", "dp", "tensor"),
        P("expert", "dp", "tensor"),
        P("expert", "tensor", "dp"),
    )
    return jax.shard_map(
        local,
        mesh=mesh,
        in_specs=placed,
        out_specs=(
            P("expert", "dp", "tensor"),
            P("expert", "dp", "tensor"),
            P("expert", "tensor", "dp"),
            P(("dp", "expert"), None),
        ),
        check_vma=False,
    )
```

profile of v0, /device:TPU:1, one launch (start us, length us, event | category | flops | bytes accessed | tf_op | source)
XLA Modules:
  0.0 616.6 jit_solution(12437453717802722302)
XLA Ops:
  7.2 0.9 copy.28
  8.1 0.1 eq.59
  8.4 1.2 reduce-window.6
  9.6 0.2 slice_reduce_fusion
  9.8 0.2 reduce-window.9
  10.1 0.1 reduce_sum.48
  10.3 0.7 multiply_add_fusion
  11.1 8.8 %fusion.5 = bf16[768,3584]{1,0:T(8,128)(2,1)} fusion(bf16[1,768,3584]{2,1,0:T(8,128)(2,1)} %param.10, bf16[1,768,3584]{2,1,0:T(8,128)(2,1)} %param.9), kind=kLoop, calls=%fused_computation.13 | loop fusion | flops 22020096 | bytes 16515072 | tf_op jit(solution)/shard_map/convert_element_type | solution.py:44
  19.9 0.8 convolution_convert_fusion.2
  20.7 23.2 %all_to_all.20 = bf16[4,192,1024]{2,1,0:T(8,128)(2,1)} all-to-all(bf16[4,192,1024]{2,1,0:T(8,128)(2,1)S(1)} %bitcast.61), channel_id=1, replica_groups=mesh['dp'=2,'expert'=4,'tensor'=4] {'expert'}, dimensions={0} | all-to-all | bytes 3145728 | tf_op jit(solution)/shard_map/all_to_all | solution.py:53
  44.0 1.8 collective-permute-start
  45.7 115.1 %all-gather.3.cloned.1.call-done = bf16[768,4096]{1,0:T(8,128)(2,1)} async-done(((bf16[768,1024]{1,0:T(8,128)(2,1)}), bf16[768,4096]{1,0:T(8,128)(2,1)}) %all-gather.3.cloned.1.call-update) | async-done | bytes 6291472 | tf_op jit(solution)/shard_map/all_gather | solution.py:59
  160.8 1.2 constant_dynamic-slice_fusion
  162.0 1.2 collective-permute-start.1
  163.2 18.3 %collective-permute-done.1 = bf16[768,512]{1,0:T(8,128)(2,1)S(1)} collective-permute-done((bf16[768,512]{1,0:T(8,128)(2,1)S(1)}, bf16[768,512]{1,0:T(8,128)(2,1)S(1)}, u32[]{:S(2)}, u32[]{:S(2)}) %collective-permute-start.1) | collective-permute-done | bytes 786464 | tf_op jit(solution)/shard_map/ppermute | solution.py:15
  181.5 0.9 copy-done.2
  182.5 64.6 %all-gather.5.cloned.1.call-done = bf16[768,2048]{1,0:T(8,128)(2,1)} async-done(((bf16[768,512]{1,0:T(8,128)(2,1)}), bf16[768,2048]{1,0:T(8,128)(2,1)}) %all-gather.5.cloned.1.call-update) | async-done | bytes 3145744 | tf_op jit(solution)/shard_map/all_gather | solution.py:68
  247.0 18.2 %fusion.1 = f32[768,3584]{1,0:T(8,128)} fusion(bf16[768,2048]{1,0:T(8,128)(2,1)} %all-gather.5.cloned.1.call-done, bf16[1,3584,2048]{2,1,0:T(8,128)(2,1)} %param.11), kind=kOutput, calls=%fused_computation.7 | convolution fusion | flops 11274289152 | bytes 28835840 | tf_op jit(solution)/shard_map/dot_general | solution.py:72
  265.2 1.2 collective-permute-start.2
  266.4 0.2 select_reduce_fusion.2
  266.7 7.0 %all_to_all.21 = bf16[4,1,192]{2,1,0:T(2,128)(2,1)S(1)} all-to-all(bf16[4,1,192]{2,1,0:T(2,128)(2,1)S(1)} %convert_element_type.113), channel_id=1, replica_groups=mesh['dp'=2,'expert'=4,'tensor'=4] {'expert'}, dimensions={0} | all-to-all | bytes 3072 | tf_op jit(solution)/shard_map/all_to_all | solution.py:54
  273.8 0.3 collective-permute-start.3
  274.1 229.0 %collective-permute-done.3 = bf16[768]{0:T(1024)(128)(2,1)S(1)} collective-permute-done((bf16[768]{0:T(1024)(128)(2,1)S(1)}, bf16[768]{0:T(1024)(128)(2,1)S(1)}, u32[]{:S(2)}, u32[]{:S(2)}) %collective-permute-start.3) | collective-permute-done | bytes 1568 | tf_op jit(solution)/shard_map/ppermute | solution.py:15
  503.1 18.3 %convolution_convert_fusion.1 = bf16[3584,2048]{1,0:T(8,128)(2,1)} fusion(bf16[768,3584]{1,0:T(8,128)(2,1)} %fusion.5, f32[768]{0:T(1024)S(1)} %convert_element_type.91, bf16[768,4096]{1,0:T(8,128)(2,1)} %all-gather.3.cloned.1.call-done, s32[]{:T(128)S(6)} %select_n.31), kind=kOutput, calls=%fused_computation.5 | convolution fusion | flops 11286347776 | bytes 23333892 | tf_op jit(solution)/shard_map/dot_general | solution.py:81
  521.3 18.3 %fusion.3 = f32[768,3584]{1,0:T(8,128)} fusion(bf16[1,3584,2048]{2,1,0:T(8,128)(2,1)} %param.11, bf16[768,4096]{1,0:T(8,128)(2,1)} %all-gather.3.cloned.1.call-done, s32[]{:T(128)S(6)} %select_n.31), kind=kOutput, calls=%fused_computation.9 | convolution fusion | flops 11274289152 | bytes 28835844 | tf_op jit(solution)/shard_map/dot_general | solution.py:76
  539.6 17.9 %convolution_convert_fusion = bf16[3584,2048]{1,0:T(8,128)(2,1)} fusion(bf16[768,3584]{1,0:T(8,128)(2,1)} %collective-permute-done, bf16[768,2048]{1,0:T(8,128)(2,1)} %all-gather.5.cloned.1.call-done, f32[768]{0:T(1024)S(1)} %convert_element_type.101), kind=kOutput, calls=%fused_computation.4 | convolution fusion | flops 11286347776 | bytes 23333888 | tf_op jit(solution)/shard_map/dot_general | solution.py:84
  557.5 17.8 %fusion.13 = (bf16[1,768,3584]{2,1,0:T(8,128)(2,1)}, bf16[1,768,3584]{2,1,0:T(8,128)(2,1)}, f32[768]{0:T(1024)S(1)}) fusion(f32[768]{0:T(1024)S(1)} %convert_element_type.91, bf16[1,768,3584]{2,1,0:T(8,128)(2,1)S(1)} %bitcast.59, f32[768,3584]{1,0:T(8,128)} %fusion.3, f32[768,3584]{1,0:T(8,128)} %collective-permute-done.2, bf16[1,768,3584]{2,1,0:T(8,128)(2,1)} %param.10, ...), kind=kLoop, calls=%fused_computation.25 | loop fusion | flops 55049472 | bytes 49551360 | tf_op jit(solution)/shard_map/broadcast_in_dim | solution.py:116
  575.4 8.4 %psum.7 = f32[4,1,192]{2,1,0:T(1,128)} all-reduce(f32[4,1,192]{2,1,0:T(1,128)S(1)} %all_to_all.15), channel_id=1, replica_groups=mesh['dp'=2,'expert'=4,'tensor'=4] {'tensor'}, use_global_device_ids=true, to_apply=%region_5.6 | all-reduce | flops 768 | bytes 6144 | tf_op jit(solution)/shard_map/psum | solution.py:100
  583.9 6.2 %all-to-all-start.2 = ((f32[4,1,192]{2,1,0:T(1,128)}), f32[4,1,192]{2,1,0:T(1,128)S(1)}, u32[]{:S(2)}, u32[]{:S(2)}) async-start(f32[4,1,192]{2,1,0:T(1,128)} %psum.7), calls=%async_computation.2 | async-start | bytes 8192 | tf_op jit(solution)/shard_map/all_to_all | solution.py:101
  590.1 18.7 %fusion = bf16[1,3584,2048]{2,1,0:T(8,128)(2,1)} fusion(bf16[3584,2048]{1,0:T(8,128)(2,1)} %convolution_convert_fusion, bf16[3584,2048]{1,0:T(8,128)(2,1)} %convolution_convert_fusion.1), kind=kLoop, calls=%fused_computation.6 | loop fusion | flops 29360128 | bytes 44040192 | tf_op jit(solution)/shard_map/broadcast_in_dim | solution.py:116
  608.8 0.3 select_reduce_fusion.1
  609.2 0.6 pad_maximum_fusion
  (34 shorter events, 0.9 us)
Async XLA Ops:
  7.2 12.7 %copy-start = (bf16[256,1024]{1,0:T(8,128)(2,1)S(1)}, bf16[256,1024]{1,0:T(8,128)(2,1)}, u32[]{:S(2)}) copy-start(bf16[256,1024]{1,0:T(8,128)(2,1)} %param.6) | copy-start | bytes 1572868
  7.2 153.6 %all-gather.3.cloned.1.call-start = ((), (), s32[]{:S(2)}) async-start(), calls=%async_computation.3 | async-start | bytes 7864320 | tf_op jit(solution)/shard_map/all_gather | solution.py:59
  43.9 203.1 %all-gather.5.cloned.1.call-start = ((), (), s32[]{:S(2)}) async-start(), calls=%async_computation.4 | async-start | bytes 3932160 | tf_op jit(solution)/shard_map/all_gather | solution.py:68
  44.0 138.5 %collective-permute-start = (bf16[768,3584]{1,0:T(8,128)(2,1)}, bf16[768,3584]{1,0:T(8,128)(2,1)}, u32[]{:S(2)}, u32[]{:S(2)}) collective-permute-start(bf16[768,3584]{1,0:T(8,128)(2,1)} %fusion.5), channel_id=1, source_target_pairs={{0,16},{16,0},{1,17},{17,1},{2,18},{18,2},{3,19},{19,3},{4,20},{20... | collective-permute-start | bytes 16515080 | tf_op jit(solution)/shard_map/ppermute | solution.py:15
  162.0 19.6 %collective-permute-start.1 = (bf16[768,512]{1,0:T(8,128)(2,1)S(1)}, bf16[768,512]{1,0:T(8,128)(2,1)S(1)}, u32[]{:S(2)}, u32[]{:S(2)}) collective-permute-start(bf16[768,512]{1,0:T(8,128)(2,1)S(1)} %constant_dynamic-slice_fusion), channel_id=1, source_target_pairs={{0,16},{16,0},{1,17},{17,1},{2,18},{18,2},{3,19},{19,3},{4,20},{20... | collective-permute-start | bytes 2359304 | tf_op jit(solution)/shard_map/ppermute | solution.py:15
  181.5 0.9 copy-start.2
  182.4 83.9 %copy-start.3 = (bf16[256,2]{0,1:T(2,128)(2,1)S(1)}, bf16[256,2]{0,1:T(2,128)(2,1)}, u32[]{:S(2)}) copy-start(bf16[256,2]{0,1:T(2,128)(2,1)} %param.8) | copy-start | bytes 3076
  265.2 292.3 %collective-permute-start.2 = (f32[768,3584]{1,0:T(8,128)}, f32[768,3584]{1,0:T(8,128)}, u32[]{:S(2)}, u32[]{:S(2)}) collective-permute-start(f32[768,3584]{1,0:T(8,128)} %fusion.1), channel_id=1, source_target_pairs={{0,16},{16,0},{1,17},{17,1},{2,18},{18,2},{3,19},{19,3},{4,20},{20... | collective-permute-start | bytes 33030152 | tf_op jit(solution)/shard_map/ppermute | solution.py:15
  273.8 229.3 %collective-permute-start.3 = (bf16[768]{0:T(1024)(128)(2,1)S(1)}, bf16[768]{0:T(1024)(128)(2,1)S(1)}, u32[]{:S(2)}, u32[]{:S(2)}) collective-permute-start(bf16[768]{0:T(1024)(128)(2,1)S(1)} %reshape.71), channel_id=1, source_target_pairs={{0,16},{16,0},{1,17},{17,1},{2,18},{18,2},{3,19},{19,3},{4,20},{20... | collective-permute-start | bytes 4616 | tf_op jit(solution)/shard_map/ppermute | solution.py:15
  503.1 54.5 %slice-start = ((s8[5505024]{0:T(1024)(128)(4,1)}), s8[4194304]{0:T(1024)(128)(4,1)S(1)}, s32[]{:S(2)}) async-start(s8[5505024]{0:T(1024)(128)(4,1)} %bitcast.58), calls=%async_computation.5 | async-start | bytes 8388608
  521.3 36.2 %slice-start.1 = ((s8[5505024]{0:T(1024)(128)(4,1)}), s8[1310720]{0:T(1024)(128)(4,1)S(1)}, s32[]{:S(2)}) async-start(s8[5505024]{0:T(1024)(128)(4,1)} %bitcast.58), calls=%async_computation.6 | async-start | bytes 2621440
  583.9 24.9 %all-to-all-start.2 = ((f32[4,1,192]{2,1,0:T(1,128)}), f32[4,1,192]{2,1,0:T(1,128)S(1)}, u32[]{:S(2)}, u32[]{:S(2)}) async-start(f32[4,1,192]{2,1,0:T(1,128)} %psum.7), calls=%async_computation.2 | async-start | bytes 8192 | tf_op jit(solution)/shard_map/all_to_all | solution.py:101
  590.1 19.7 %copy-start.1 = (bf16[256,1024]{1,0:T(8,128)(2,1)S(1)}, bf16[256,1024]{1,0:T(8,128)(2,1)}, u32[]{:S(2)}) copy-start(bf16[256,1024]{1,0:T(8,128)(2,1)} %param.6) | copy-start | bytes 1572868
Sparse Core Ops, SparseCore 0:
  44.1 116.7 all-gather.2
  182.6 64.4 all-gather.4
where the time goes:
time: 617 us
  waiting for transfers between devices  427 us (69%)
  matrix products  73.4 us (12%)
  other arithmetic  48.8 us (8%)
  blocking collectives  38.6 us (6%)
  between operations  14.1 us (2%)
  starting transfers between devices  10.7 us (2%)
    ppermute x4, waiting for transfers between devices, swap_dp(): return lax.ppermute(value, 'dp', perm=[(0, 1), (1, 0)])  247 us
    all_gather x1, waiting for transfers between devices, local(): fragment = lax.all_gather(narrow_rows, 'tensor', axis=1, tiled=True)  115 us
    all_gather x1, waiting for transfers between devices, local(): other_rows = lax.all_gather(other_piece, 'tensor', axis=1, tiled=True)  64.6 us
    broadcast_in_dim x2, other arithmetic, local(): return (gate_grad[None], up_grad[None], down_grad[None], router_grad)  36.5 us
    all_to_all x1, blocking collectives, local(): lax.all_to_all(outgoing, 'expert', split_axis=0, concat_axis=0, tiled=True)  23.2 us
    dot_general x1, matrix products, local(): lax.dot_general(own_rows, local_weight, contract_cols, preferred_element_...  18.3 us
    dot_general x1, matrix products, local(): lax.dot_general(hidden, scaled_own, contract_rows, preferred_element_type...  18.3 us
    dot_general x1, matrix products, local(): lax.dot_general(other_rows, local_weight, contract_cols, preferred_elemen...  18.2 us
  transfers between devices with their start and end apart: 7, of which 4 were waited for; matrix products, arithmetic and copies ran while one was open for 12% of the time, Pallas kernels for 0%

commit v1 on v0

--- a/solution.py
+++ b/solution.py
@@ -4,6 +4,22 @@
 from jax.sharding import PartitionSpec as P
 
 PARTIAL_DTYPE = jnp.float32
+
+
+def swapped_with_each(array, axis, split, join):
+    ways, here = (lax.axis_size(axis), lax.axis_index(axis))
+    width = array.shape[split] // ways
+    lengths = list(array.shape)
+    lengths[split] = width
+    height = lengths[join]
+    lengths[join] = height * ways
+    full = jnp.zeros(lengths, array.dtype)
+    for mask in range(ways):
+        part = lax.dynamic_slice_in_dim(array, (here ^ mask) * width, width, axis=split)
+        if mask:
+            part = lax.ppermute(part, axis, [(d, d ^ mask) for d in range(ways)])
+        full = lax.dynamic_update_slice_in_dim(full, part, (here ^ mask) * height, axis=join)
+    return full
 
 
 def silu_parts(values):
@@ -50,7 +66,7 @@
     outgoing = outgoing.astype(jnp.bfloat16).reshape(expert_count, capacity, -1)
     hidden, outgoing = lax.optimization_barrier((hidden, outgoing))
     hidden_other = swap_dp(hidden)
-    received = lax.all_to_all(outgoing, "expert", split_axis=0, concat_axis=0, tiled=True)
+    received = swapped_with_each(outgoing, "expert", 0, 0)
     gate_slots = lax.all_to_all(gate_send, "expert", split_axis=0, concat_axis=0, tiled=True)
     slots = expert_count * capacity
     narrow_rows = received.reshape(slots, -1)

time: 617 us -> 607 us (0.984)
  blocking collectives: 38.6 us -> 15.4 us
  waiting for transfers between devices: 427 us -> 445 us
  other arithmetic: 48.8 us -> 30.9 us
  matrix products: 73.4 us -> 80.1 us
    all_to_all x1 -> x0, blocking collectives: 23.2 us -> none  [local(): lax.all_to_all(outgoing, 'expert', split_axis=0, concat_axis=0, tiled=True)]
    broadcast_in_dim x2 -> x1, other arithmetic: 36.5 us -> 18.7 us  [local(): return (gate_grad[None], up_grad[None], down_grad[None], router_grad)]
    ppermute x0 -> x3, waiting for transfers between devices: none -> 17.7 us  [swapped_with_each(): part = lax.ppermute(part, axis, [(d, d ^ mask) for d in range(ways)])]
    dot_general x1, matrix products: 18.3 us -> 24.8 us  [local(): lax.dot_general(own_rows, local_weight, contract_cols, preferred_element_...]
  transfers between devices with their start and end apart: 7 -> 10, of which waited for: 4 -> 6; matrix products, arithmetic and copies ran while one was open for 12% -> 9% of each run, Pallas kernels for 0% -> 0%
where the time goes in v1:
time: 607 us; the launch traced here: 606 us
  waiting for transfers between devices  445 us (73%)
  matrix products  80.1 us (13%)
  other arithmetic  30.9 us (5%)
  blocking collectives  15.4 us (3%)
  between operations  14.2 us (2%)
  starting transfers between devices  13.3 us (2%)
  local copies, waits for them, and re-layouts  6.91 us (1%)
    ppermute x4, waiting for transfers between devices, swap_dp(): return lax.ppermute(value, 'dp', perm=[(0, 1), (1, 0)])  247 us
    all_gather x1, waiting for transfers between devices, local(): fragment = lax.all_gather(narrow_rows, 'tensor', axis=1, tiled=True)  115 us
    all_gather x1, waiting for transfers between devices, local(): other_rows = lax.all_gather(other_piece, 'tensor', axis=1, tiled=True)  65.4 us
    dot_general x1, matrix products, local(): lax.dot_general(own_rows, local_weight, contract_cols, preferred_element_...  24.8 us
    broadcast_in_dim x1, other arithmetic, local(): return (gate_grad[None], up_grad[None], down_grad[None], router_grad)  18.7 us
    dot_general x1, matrix products, local(): lax.dot_general(hidden, scaled_own, contract_rows, preferred_element_type...  18.3 us
    dot_general x1, matrix products, local(): lax.dot_general(other_rows, local_weight, contract_cols, preferred_elemen...  18.2 us
    ppermute x3, waiting for transfers between devices, swapped_with_each(): part = lax.ppermute(part, axis, [(d, d ^ mask) for d in range(ways)])  17.7 us
  transfers between devices with their start and end apart: 10, of which 6 were waited for; matrix products, arithmetic and copies ran while one was open for 9% of the time, Pallas kernels for 0%

profile of v1, /device:TPU:1, one launch (start us, length us, event | category | flops | bytes accessed | tf_op | source)
XLA Modules:
  0.0 606.2 jit_solution(898286910435385008)
XLA Ops:
  7.2 0.9 copy.28
  8.4 1.2 reduce-window.6
  9.6 0.2 slice_reduce_fusion
  10.4 0.7 multiply_add_fusion
  11.1 8.8 %fusion.5 = bf16[768,3584]{1,0:T(8,128)(2,1)} fusion(bf16[1,768,3584]{2,1,0:T(8,128)(2,1)} %param.10, bf16[1,768,3584]{2,1,0:T(8,128)(2,1)} %param.9), kind=kLoop, calls=%fused_computation.13 | loop fusion | flops 22020096 | bytes 16515072 | tf_op jit(solution)/shard_map/convert_element_type | solution.py:60
  19.9 1.9 convolution_convert_fusion.2
  22.0 1.5 constant_dynamic-slice_fusion.1
  23.6 2.7 collective-permute-start.1
  26.4 9.3 %collective-permute-done.1 = bf16[1,192,1024]{2,1,0:T(8,128)(2,1)S(1)} collective-permute-done((bf16[1,192,1024]{2,1,0:T(8,128)(2,1)S(1)}, bf16[1,192,1024]{2,1,0:T(8,128)(2,1)S(1)}, u32[]{:S(2)}, u32[]{:S(2)}) %collective-permute-start.1) | collective-permute-done | bytes 393248 | tf_op jit(solution)/shard_map/ppermute | solution.py:20
  35.8 8.4 %collective-permute-done.2 = bf16[1,192,1024]{2,1,0:T(8,128)(2,1)S(1)} collective-permute-done((bf16[1,192,1024]{2,1,0:T(8,128)(2,1)S(1)}, bf16[1,192,1024]{2,1,0:T(8,128)(2,1)S(1)}, u32[]{:S(2)}, u32[]{:S(2)}) %collective-permute-start.2) | collective-permute-done | bytes 393248 | tf_op jit(solution)/shard_map/ppermute | solution.py:20
  44.2 1.1 copy-done.2
  45.4 1.5 collective-permute-start.3
  46.9 115.2 %all-gather.3.cloned.1.call-done = bf16[768,4096]{1,0:T(8,128)(2,1)} async-done(((bf16[768,1024]{1,0:T(8,128)(2,1)}), bf16[768,4096]{1,0:T(8,128)(2,1)}) %all-gather.3.cloned.1.call-update) | async-done | bytes 6291472 | tf_op jit(solution)/shard_map/all_gather | solution.py:75
  162.1 1.2 constant_dynamic-slice_fusion
  163.3 1.2 collective-permute-start.4
  164.6 18.1 %collective-permute-done.4 = bf16[768,512]{1,0:T(8,128)(2,1)S(1)} collective-permute-done((bf16[768,512]{1,0:T(8,128)(2,1)S(1)}, bf16[768,512]{1,0:T(8,128)(2,1)S(1)}, u32[]{:S(2)}, u32[]{:S(2)}) %collective-permute-start.4) | collective-permute-done | bytes 786464 | tf_op jit(solution)/shard_map/ppermute | solution.py:31
  182.6 0.9 copy-done.3
  183.6 65.4 %all-gather.5.cloned.1.call-done = bf16[768,2048]{1,0:T(8,128)(2,1)} async-done(((bf16[768,512]{1,0:T(8,128)(2,1)}), bf16[768,2048]{1,0:T(8,128)(2,1)}) %all-gather.5.cloned.1.call-update) | async-done | bytes 3145744 | tf_op jit(solution)/shard_map/all_gather | solution.py:84
  248.9 18.2 %fusion.1 = f32[768,3584]{1,0:T(8,128)} fusion(bf16[768,2048]{1,0:T(8,128)(2,1)} %all-gather.5.cloned.1.call-done, bf16[1,3584,2048]{2,1,0:T(8,128)(2,1)} %param.11), kind=kOutput, calls=%fused_computation.7 | convolution fusion | flops 11274289152 | bytes 28835840 | tf_op jit(solution)/shard_map/dot_general | solution.py:88
  267.1 1.2 collective-permute-start.5
  268.3 0.2 select_reduce_fusion.2
  268.6 7.0 %all_to_all.15 = bf16[4,1,192]{2,1,0:T(2,128)(2,1)S(1)} all-to-all(bf16[4,1,192]{2,1,0:T(2,128)(2,1)S(1)} %convert_element_type.113), channel_id=1, replica_groups=mesh['dp'=2,'expert'=4,'tensor'=4] {'expert'}, dimensions={0} | all-to-all | bytes 3072 | tf_op jit(solution)/shard_map/all_to_all | solution.py:70
  275.7 0.3 collective-permute-start.6
  276.0 229.0 %collective-permute-done.6 = bf16[768]{0:T(1024)(128)(2,1)S(1)} collective-permute-done((bf16[768]{0:T(1024)(128)(2,1)S(1)}, bf16[768]{0:T(1024)(128)(2,1)S(1)}, u32[]{:S(2)}, u32[]{:S(2)}) %collective-permute-start.6) | collective-permute-done | bytes 1568 | tf_op jit(solution)/shard_map/ppermute | solution.py:31
  505.0 18.3 %convolution_convert_fusion.1 = bf16[3584,2048]{1,0:T(8,128)(2,1)} fusion(bf16[768,3584]{1,0:T(8,128)(2,1)} %fusion.5, f32[768]{0:T(1024)S(1)} %convert_element_type.91, bf16[768,4096]{1,0:T(8,128)(2,1)} %all-gather.3.cloned.1.call-done, s32[]{:T(128)S(6)} %select_n.51), kind=kOutput, calls=%fused_computation.5 | convolution fusion | flops 11286347776 | bytes 23333892 | tf_op jit(solution)/shard_map/dot_general | solution.py:97
  523.3 16.9 %convolution_convert_fusion = bf16[3584,2048]{1,0:T(8,128)(2,1)} fusion(bf16[768,3584]{1,0:T(8,128)(2,1)} %collective-permute-done.3, bf16[768,2048]{1,0:T(8,128)(2,1)S(1)} %copy-done.5, f32[768]{0:T(1024)S(1)} %convert_element_type.101), kind=kOutput, calls=%fused_computation.4 | convolution fusion | flops 11286347776 | bytes 23333888 | tf_op jit(solution)/shard_map/dot_general | solution.py:100
  540.2 24.8 %fusion.16 = (bf16[1,768,3584]{2,1,0:T(8,128)(2,1)}, bf16[1,768,3584]{2,1,0:T(8,128)(2,1)}, f32[768]{0:T(1024)S(1)}) fusion(f32[768]{0:T(1024)S(1)} %convert_element_type.91, bf16[1,768,3584]{2,1,0:T(8,128)(2,1)} %param.9, bf16[1,768,3584]{2,1,0:T(8,128)(2,1)} %param.10, bf16[768,3584]{1,0:T(8,128)(2,1)} %fusion.5, f32[768,3584]{1,0:T(8,128)} %collective-permute-done.5, ...), kind=kOutput, calls=%fused_computation.26 | convolution fusion | flops 11329338368 | bytes 56367108 | tf_op jit(solution)/shard_map/dot_general | solution.py:92
  565.1 8.4 %psum.7 = f32[4,1,192]{2,1,0:T(1,128)} all-reduce(f32[4,1,192]{2,1,0:T(1,128)S(1)} %all_to_all.11), channel_id=1, replica_groups=mesh['dp'=2,'expert'=4,'tensor'=4] {'tensor'}, use_global_device_ids=true, to_apply=%region_5.6 | all-reduce | flops 768 | bytes 6144 | tf_op jit(solution)/shard_map/psum | solution.py:116
  573.5 6.2 %all-to-all-start.1 = ((f32[4,1,192]{2,1,0:T(1,128)}), f32[4,1,192]{2,1,0:T(1,128)S(1)}, u32[]{:S(2)}, u32[]{:S(2)}) async-start(f32[4,1,192]{2,1,0:T(1,128)} %psum.7), calls=%async_computation.1 | async-start | bytes 8192 | tf_op jit(solution)/shard_map/all_to_all | solution.py:117
  579.7 18.7 %fusion = bf16[1,3584,2048]{2,1,0:T(8,128)(2,1)} fusion(bf16[3584,2048]{1,0:T(8,128)(2,1)} %convolution_convert_fusion, bf16[3584,2048]{1,0:T(8,128)(2,1)} %convolution_convert_fusion.1), kind=kLoop, calls=%fused_computation.6 | loop fusion | flops 29360128 | bytes 44040192 | tf_op jit(solution)/shard_map/broadcast_in_dim | solution.py:132
  598.5 0.3 select_reduce_fusion.1
  598.8 0.6 pad_maximum_fusion
  (42 shorter events, 1.8 us)
Async XLA Ops:
  7.2 12.8 %copy-start = (bf16[256,1024]{1,0:T(8,128)(2,1)S(1)}, bf16[256,1024]{1,0:T(8,128)(2,1)}, u32[]{:S(2)}) copy-start(bf16[256,1024]{1,0:T(8,128)(2,1)} %param.6) | copy-start | bytes 1572868
  7.2 154.9 %all-gather.3.cloned.1.call-start = ((), (), s32[]{:S(2)}) async-start(), calls=%async_computation.2 | async-start | bytes 7864320 | tf_op jit(solution)/shard_map/all_gather | solution.py:75
  23.5 2.9 collective-permute-start
  23.6 12.1 %collective-permute-start.1 = (bf16[1,192,1024]{2,1,0:T(8,128)(2,1)S(1)}, bf16[1,192,1024]{2,1,0:T(8,128)(2,1)S(1)}, u32[]{:S(2)}, u32[]{:S(2)}) collective-permute-start(bf16[1,192,1024]{2,1,0:T(8,128)(2,1)S(1)} %get-tuple-element.24), channel_id=1, source_target_pairs={{0,8},{4,12},{8,0},{12,4},{1,9},{5,13},{9,1},{13,5},{2,10},{6,14},... | collective-permute-start | bytes 1179656 | tf_op jit(solution)/shard_map/ppermute | solution.py:20
  26.3 17.8 %collective-permute-start.2 = (bf16[1,192,1024]{2,1,0:T(8,128)(2,1)S(1)}, bf16[1,192,1024]{2,1,0:T(8,128)(2,1)S(1)}, u32[]{:S(2)}, u32[]{:S(2)}) collective-permute-start(bf16[1,192,1024]{2,1,0:T(8,128)(2,1)S(1)} %get-tuple-element.23), channel_id=1, source_target_pairs={{0,12},{4,8},{8,4},{12,0},{1,13},{5,9},{9,5},{13,1},{2,14},{6,10},... | collective-permute-start | bytes 1179656 | tf_op jit(solution)/shard_map/ppermute | solution.py:20
  44.2 1.1 copy-start.2
  45.4 203.6 %all-gather.5.cloned.1.call-start = ((), (), s32[]{:S(2)}) async-start(), calls=%async_computation.3 | async-start | bytes 3932160 | tf_op jit(solution)/shard_map/all_gather | solution.py:84
  45.4 138.1 %collective-permute-start.3 = (bf16[768,3584]{1,0:T(8,128)(2,1)}, bf16[768,3584]{1,0:T(8,128)(2,1)}, u32[]{:S(2)}, u32[]{:S(2)}) collective-permute-start(bf16[768,3584]{1,0:T(8,128)(2,1)} %fusion.5), channel_id=1, source_target_pairs={{0,16},{16,0},{1,17},{17,1},{2,18},{18,2},{3,19},{19,3},{4,20},{20... | collective-permute-start | bytes 16515080 | tf_op jit(solution)/shard_map/ppermute | solution.py:31
  163.3 19.3 %collective-permute-start.4 = (bf16[768,512]{1,0:T(8,128)(2,1)S(1)}, bf16[768,512]{1,0:T(8,128)(2,1)S(1)}, u32[]{:S(2)}, u32[]{:S(2)}) collective-permute-start(bf16[768,512]{1,0:T(8,128)(2,1)S(1)} %constant_dynamic-slice_fusion), channel_id=1, source_target_pairs={{0,16},{16,0},{1,17},{17,1},{2,18},{18,2},{3,19},{19,3},{4,20},{20... | collective-permute-start | bytes 2359304 | tf_op jit(solution)/shard_map/ppermute | solution.py:31
  182.6 0.9 copy-start.3
  183.5 84.8 %copy-start.4 = (bf16[256,2]{0,1:T(2,128)(2,1)S(1)}, bf16[256,2]{0,1:T(2,128)(2,1)}, u32[]{:S(2)}) copy-start(bf16[256,2]{0,1:T(2,128)(2,1)} %param.8) | copy-start | bytes 3076
  267.1 273.0 %collective-permute-start.5 = (f32[768,3584]{1,0:T(8,128)}, f32[768,3584]{1,0:T(8,128)}, u32[]{:S(2)}, u32[]{:S(2)}) collective-permute-start(f32[768,3584]{1,0:T(8,128)} %fusion.1), channel_id=1, source_target_pairs={{0,16},{16,0},{1,17},{17,1},{2,18},{18,2},{3,19},{19,3},{4,20},{20... | collective-permute-start | bytes 33030152 | tf_op jit(solution)/shard_map/ppermute | solution.py:31
  275.7 229.3 %collective-permute-start.6 = (bf16[768]{0:T(1024)(128)(2,1)S(1)}, bf16[768]{0:T(1024)(128)(2,1)S(1)}, u32[]{:S(2)}, u32[]{:S(2)}) collective-permute-start(bf16[768]{0:T(1024)(128)(2,1)S(1)} %reshape.71), channel_id=1, source_target_pairs={{0,16},{16,0},{1,17},{17,1},{2,18},{18,2},{3,19},{19,3},{4,20},{20... | collective-permute-start | bytes 4616 | tf_op jit(solution)/shard_map/ppermute | solution.py:31
  505.0 18.3 %copy-start.5 = (bf16[768,2048]{1,0:T(8,128)(2,1)S(1)}, bf16[768,2048]{1,0:T(8,128)(2,1)}, u32[]{:S(2)}) copy-start(bf16[768,2048]{1,0:T(8,128)(2,1)} %all-gather.5.cloned.1.call-done) | copy-start | bytes 9437188
  573.5 24.9 %all-to-all-start.1 = ((f32[4,1,192]{2,1,0:T(1,128)}), f32[4,1,192]{2,1,0:T(1,128)S(1)}, u32[]{:S(2)}, u32[]{:S(2)}) async-start(f32[4,1,192]{2,1,0:T(1,128)} %psum.7), calls=%async_computation.1 | async-start | bytes 8192 | tf_op jit(solution)/shard_map/all_to_all | solution.py:117
  579.7 19.7 %copy-start.1 = (bf16[256,1024]{1,0:T(8,128)(2,1)S(1)}, bf16[256,1024]{1,0:T(8,128)(2,1)}, u32[]{:S(2)}) copy-start(bf16[256,1024]{1,0:T(8,128)(2,1)} %param.6) | copy-start | bytes 1572868
Sparse Core Ops, SparseCore 0:
  45.5 116.5 all-gather.2
  183.7 65.2 all-gather.4
